TPU v7x, 256 devices: a whole 4x4x8 slice. The times are simulated.
256 devices in a mesh: seq: 64 (over x, z, core), ch: 4 (over y).
Axes of the slice: x: 4, y: 4, z: 8, core: 2. Of those that a mesh axis runs over, the one named last changes fastest.
Arguments:
- inputs: bfloat16 [8192, 4096], P('seq'), may hold values from -6 to 6
- norm_gain: float32 [4096], replicated, may hold values from 0.1 to 1.9
- in_weight: bfloat16 [4096, 3, 1024], P('seq', None, 'ch'), may hold values from -0.09375 to 0.09375
- short_filter: float32 [3, 3, 1024], P(None, None, 'ch'), may hold values from -4 to 4
- long_filter: float32 [8192, 1024], P('seq', 'ch'), may hold values from -2.2 to 2.2
- conv_bias: float32 [1024], P('ch'), may hold values from -4 to 4
- out_weight: bfloat16 [1024, 4096], P('ch', 'seq'), may hold values from -0.1875 to 0.1875
- out_grad: bfloat16 [8192, 4096], P('seq'), may hold values from -6 to 6
Outputs:
- block_out: bfloat16 [8192, 4096], P('seq', 'ch')
- in_grad: bfloat16 [8192, 4096], P('seq')
- filter_grad: float32 [8192, 1024], P('seq', 'ch')
All inputs are finite; a program needn't handle non-finite values.
Results may differ from a plain program's by a relative error of at most 0.013.
Values may be sent and summed in bfloat16 or wider, within the bound.
No kernel may reach another device: no remote copies, remote signals or barrier semaphores. Data moves between devices by JAX's collectives and lax.ppermute only.
A program may use at most 64 MiB of HBM per device.

v0:
```python
import math
import jax
import jax.numpy as jnp
from jax import lax
from jax.sharding import PartitionSpec as P

epsilon = 1e-05
highest = lax.Precision.HIGHEST


def passed_along(block, axis, distance):
    devices = range(lax.axis_size(axis))
    route = [(i - distance, i) for i in devices if i - distance in devices]
    return lax.ppermute(block, axis, route)


def doubled_gather(block, axis):
    devices = lax.axis_size(axis)
    place = lax.axis_index(axis)
    bits = devices.bit_length() - 1
    assert 1 << bits == devices
    gathered = block
    for bit in reversed(range(bits)):
        route = [(i, i ^ 1 << bit) for i in range(devices)]
        arrived = lax.ppermute(gathered, axis, route)
        lower = place >> bit & 1 == 0
        gathered = jnp.where(lower, jnp.stack([gathered, arrived]), jnp.stack([arrived, gathered]))
    gathered = gathered.transpose(tuple(reversed(range(bits))) + tuple(range(bits, gathered.ndim)))
    return gathered.reshape((devices * block.shape[0],) + block.shape[1:])


def halved_sum(partial, axis):
    devices = lax.axis_size(axis)
    place = lax.axis_index(axis)
    bits = devices.bit_length() - 1
    assert 1 << bits == devices
    rows, width = partial.shape
    share = width // devices
    held = partial.reshape((rows,) + (2,) * bits + (share,))
    held = held.transpose((0,) + tuple(range(bits, 0, -1)) + (bits + 1,)).astype(jnp.float32)
    for bit in range(bits):
        route = [(i, i ^ 1 << bit) for i in range(devices)]
        mine = place >> bit & 1
        kept = lax.dynamic_index_in_dim(held, mine, 1, keepdims=False)
        given = lax.dynamic_index_in_dim(held, 1 - mine, 1, keepdims=False)
        arrived = lax.ppermute(given.astype(jnp.bfloat16), axis, route)
        held = kept + arrived.astype(jnp.float32)
    return held


def to_columns(signals):
    return lax.all_to_all(signals, "seq", split_axis=1, concat_axis=2, tiled=True)


def to_rows(signals):
    count, chans, seq_total = signals.shape
    devices = lax.axis_size("seq")
    local_rows = seq_total // devices
    pieces = signals.reshape(count, chans, devices, local_rows).transpose(2, 0, 1, 3)
    arrived = lax.all_to_all(pieces, "seq", split_axis=0, concat_axis=0, tiled=True)
    return arrived.transpose(1, 3, 0, 2).reshape(count, local_rows, devices * chans)


def turn_table(rows, cols, period, sign):
    turns = jnp.arange(rows, dtype=jnp.int32)[:, None] * jnp.arange(cols, dtype=jnp.int32)[None, :]
    turns = lax.optimization_barrier(turns)
    phases = sign * 2.0 * math.pi / period * (turns % period).astype(jnp.float32)
    return (jnp.cos(phases), jnp.sin(phases))


def fft_sizes(seq_total):
    total = 2 * seq_total
    inner = 1
    while inner * inner < total:
        inner *= 2
    return (total // inner, inner)


def forward_dft(signals):
    count, chans, seq_total = signals.shape
    outer, inner = fft_sizes(seq_total)
    grid = signals.reshape(count, chans, outer // 2, inner)
    cos_out, sin_out = turn_table(outer, outer // 2, outer, 1.0)
    first = jnp.einsum(
        "kn,ucnm->uckm", jnp.concatenate([cos_out, -sin_out], 0), grid, precision=lax.Precision.HIGH
    )
    first_real, first_imag = (first[:, :, :outer], first[:, :, outer:])
    cos_tw, sin_tw = turn_table(outer, inner, outer * inner, 1.0)
    turned_real = first_real * cos_tw + first_imag * sin_tw
    turned_imag = first_imag * cos_tw - first_real * sin_tw
    cos_in, sin_in = turn_table(inner, inner, inner, 1.0)
    rotation = jnp.concatenate(
        [jnp.concatenate([cos_in, -sin_in], 1), jnp.concatenate([sin_in, cos_in], 1)], 0
    )
    joined = jnp.concatenate([turned_real, turned_imag], -1)
    spec = jnp.einsum("uckm,mj->uckj", joined, rotation, precision=lax.Precision.HIGH)
    return (spec[..., :inner], spec[..., inner:])


def inverse_dft(spec_real, spec_imag):
    count, chans, outer, inner = spec_real.shape
    cos_in, sin_in = turn_table(inner, inner, inner, 1.0)
    rotation = jnp.concatenate(
        [jnp.concatenate([cos_in, sin_in], 1), jnp.concatenate([-sin_in, cos_in], 1)], 0
    )
    joined = jnp.concatenate([spec_real, spec_imag], -1)
    back = jnp.einsum("uckj,jm->uckm", joined, rotation, precision=lax.Precision.HIGH)
    back_real, back_imag = (back[..., :inner], back[..., inner:])
    cos_tw, sin_tw = turn_table(outer, inner, outer * inner, 1.0)
    turned_real = back_real * cos_tw - back_imag * sin_tw
    turned_imag = back_imag * cos_tw + back_real * sin_tw
    cos_out, sin_out = turn_table(outer, outer // 2, outer, 1.0)
    grid = jnp.einsum(
        "kn,uckm->ucnm",
        jnp.concatenate([cos_out, -sin_out], 0),
        jnp.concatenate([turned_real, turned_imag], 2),
        precision=lax.Precision.HIGH,
    )
    return grid.reshape(count, chans, outer * inner // 2) / float(outer * inner)


def per_device(
    inputs, norm_gain, in_weight, short_filter, long_filter, conv_bias, out_weight, out_grad
):
    local_rows = inputs.shape[0]
    model_width = inputs.shape[1]
    slab_width = long_filter.shape[1]
    taps = short_filter.shape[1]
    wide_inputs = inputs.astype(jnp.float32)
    inv_rms = lax.rsqrt(jnp.mean(wide_inputs * wide_inputs, axis=1, keepdims=True) + epsilon)
    normed = (wide_inputs * inv_rms * norm_gain).astype(jnp.bfloat16)
    in_panel, out_panel = (
        lax.all_gather(in_weight.reshape(in_weight.shape[0], -1), "seq", axis=0, tiled=True),
        doubled_gather(out_weight.T, "seq").T,
    )
    in_flat = in_panel.reshape(model_width, 3 * slab_width)
    projected = jnp.dot(normed, in_flat, preferred_element_type=jnp.float32)
    projected = projected.astype(jnp.bfloat16).reshape(local_rows, 3, slab_width)
    upper_rim = passed_along(projected[local_rows - (taps - 1) :], "seq", 1)
    extended = jnp.concatenate([upper_rim, projected], 0).astype(jnp.float32)
    mixed = jnp.zeros((local_rows, 3, slab_width), jnp.float32)
    for offset in range(taps):
        begin = taps - 1 - offset
        mixed = mixed + short_filter[:, offset, :][None] * extended[begin : begin + local_rows]
    query_br = mixed[:, 0]
    key_br = mixed[:, 1]
    value_br = mixed[:, 2]
    product = key_br * value_br
    gate_grad = jnp.dot(out_grad, out_panel.T, preferred_element_type=jnp.float32)
    carried = gate_grad * query_br
    filt_real, filt_imag = forward_dft(to_columns(long_filter.T[None]))
    filt_real, filt_imag = (filt_real[0], filt_imag[0])
    columns = to_columns(jnp.stack([product, carried]).transpose(0, 2, 1))
    all_real, all_imag = forward_dft(columns)
    sig_real, grad_real = (all_real[0], all_real[1])
    sig_imag, grad_imag = (all_imag[0], all_imag[1])
    conv_real = sig_real * filt_real - sig_imag * filt_imag
    conv_imag = sig_real * filt_imag + sig_imag * filt_real
    back_real = grad_real * filt_real + grad_imag * filt_imag
    back_imag = grad_imag * filt_real - grad_real * filt_imag
    pair_real = grad_real * sig_real + grad_imag * sig_imag
    pair_imag = grad_imag * sig_real - grad_real * sig_imag
    outs = inverse_dft(
        jnp.stack([conv_real, back_real, pair_real]), jnp.stack([conv_imag, back_imag, pair_imag])
    )
    returned = to_rows(outs)
    conv_out = returned[0]
    back_conv = returned[1]
    filter_grad = returned[2] * float(local_rows * lax.axis_size("seq")) ** (-0.5)
    biased = conv_out + conv_bias * product
    gated = (query_br * biased).astype(jnp.bfloat16)
    partial_out = jnp.dot(gated, out_panel, preferred_element_type=jnp.float32)
    source_grad = back_conv + conv_bias * carried
    mixed_grad = jnp.stack([gate_grad * biased, source_grad * value_br, source_grad * key_br], 1)
    lower_rim = passed_along(mixed_grad[: taps - 1], "seq", -1)
    extended_back = jnp.concatenate([mixed_grad, lower_rim], 0)
    proj_grad = jnp.zeros((local_rows, 3, slab_width), jnp.float32)
    for offset in range(taps):
        proj_grad = (
            proj_grad
            + short_filter[:, offset, :][None] * extended_back[offset : offset + local_rows]
        )
    proj_grad = proj_grad.astype(jnp.bfloat16).reshape(local_rows, 3 * slab_width)
    partial_grad = jnp.dot(proj_grad, in_flat.T, preferred_element_type=jnp.float32)
    ch_size = lax.axis_size("ch")
    feature_share = model_width // ch_size
    partial_inner = jnp.sum(partial_grad * (norm_gain * wide_inputs), axis=1, keepdims=True)
    inner_high = partial_inner.astype(jnp.bfloat16)
    inner_low = (partial_inner - inner_high.astype(jnp.float32)).astype(jnp.bfloat16)
    extra = jnp.concatenate(
        [inner_high, inner_low, jnp.zeros((local_rows, 126), jnp.bfloat16)], axis=1
    )
    payload = jnp.concatenate(
        [
            partial_out.astype(jnp.bfloat16)
            .reshape(local_rows, ch_size, feature_share)
            .transpose(1, 0, 2),
            partial_grad.astype(jnp.bfloat16)
            .reshape(local_rows, ch_size, feature_share)
            .transpose(1, 0, 2),
            jnp.broadcast_to(extra[None], (ch_size, local_rows, 128)),
        ],
        axis=2,
    )
    reduced = lax.psum_scatter(payload, "ch", scatter_dimension=0).astype(jnp.float32)
    summed = reduced[:, :feature_share]
    norm_grad = reduced[:, feature_share : 2 * feature_share]
    inner_at = 2 * feature_share
    inner_term = (
        reduced[:, inner_at : inner_at + 1] + reduced[:, inner_at + 1 : inner_at + 2]
    ) / model_width
    feature_begin = lax.axis_index("ch") * feature_share
    residual = lax.dynamic_slice_in_dim(wide_inputs, feature_begin, feature_share, 1)
    block_out = (residual + summed).astype(jnp.bfloat16)
    gain_share = lax.dynamic_slice_in_dim(norm_gain, feature_begin, feature_share, 0)
    inputs_share = lax.dynamic_slice_in_dim(wide_inputs, feature_begin, feature_share, 1)
    grad_share = lax.dynamic_slice_in_dim(out_grad, feature_begin, feature_share, 1)
    weighted = norm_grad * gain_share
    in_grad_share = (
        grad_share.astype(jnp.float32) + weighted * inv_rms - inputs_share * inv_rms**3 * inner_term
    ).astype(jnp.bfloat16)
    in_grad = (
        doubled_gather(in_grad_share[None], "ch")
        .transpose(1, 0, 2)
        .reshape(local_rows, model_width)
    )
    return (block_out, in_grad, filter_grad)


def solution(mesh):
    return jax.shard_map(
        per_device,
        mesh=mesh,
        in_specs=(
            P("seq", None),
            P(),
            P("seq", None, "ch"),
            P(None, None, "ch"),
            P("seq", "ch"),
            P("ch"),
            P("ch", "seq"),
            P("seq", None),
        ),
        out_specs=(P("seq", "ch"), P("seq", None), P("seq", "ch")),
        check_vma=False,
    )
```

profile of v0, /device:TPU:2, one launch (start us, length us, event | category | flops | bytes accessed | tf_op | source)
XLA Modules:
  0.0 249.4 jit_solution(18105231908628929155)
XLA Ops:
  7.2 1.5 copy.156
  8.8 2.2 collective-permute-start.1
  11.0 1.7 copy.126
  12.6 11.2 %all-to-all-start.1 = ((f32[1,256,128]{2,0,1:T(1,128)}), f32[1,256,128]{2,0,1:T(1,128)}, u32[]{:S(2)}, u32[]{:S(2)}) async-start(f32[1,256,128]{2,0,1:T(1,128)} %bitcast.1), calls=%async_computation.1 | async-start | bytes 262144 | tf_op jit(solution)/shard_map/all_to_all | solution.py:52
  23.9 0.8 fusion.91
  24.7 0.6 iota_multiply_fusion.1
  25.4 0.8 maximum_select_fusion.8
  26.2 0.6 collective-permute-start.2
  26.8 0.8 fusion.98
  27.7 0.8 fusion.67
  28.5 2.5 %collective-permute-done.2 = bf16[2,64,256]{2,1,0:T(8,128)(2,1)S(1)} collective-permute-done((bf16[2,64,256]{2,1,0:T(8,128)(2,1)S(1)}, bf16[2,64,256]{2,1,0:T(8,128)(2,1)S(1)}, u32[]{:S(2)}, u32[]{:S(2)}) %collective-permute-start.2) | collective-permute-done | bytes 65568 | tf_op jit(solution)/shard_map/ppermute | solution.py:25
  31.0 5.2 %collective-permute-start.3 = (bf16[2,2,64,256]{3,2,0,1:T(8,128)(2,1)S(1)}, bf16[2,2,64,256]{3,2,0,1:T(8,128)(2,1)S(1)}, u32[]{:S(2)}, u32[]{:S(2)}) collective-permute-start(bf16[2,2,64,256]{3,2,0,1:T(8,128)(2,1)S(1)} %maximum_select_fusion.7), channel_id=1, source_target_pairs={{0,32},{4,36},{8,40},{12,44},{16,48},{20,52},{24,56},{28,60},{32,0... | collective-permute-start | bytes 393224 | tf_op jit(solution)/shard_map/ppermute | solution.py:25
  36.3 6.4 %collective-permute-done.3 = bf16[2,2,64,256]{3,2,0,1:T(8,128)(2,1)S(1)} collective-permute-done((bf16[2,2,64,256]{3,2,0,1:T(8,128)(2,1)S(1)}, bf16[2,2,64,256]{3,2,0,1:T(8,128)(2,1)S(1)}, u32[]{:S(2)}, u32[]{:S(2)}) %collective-permute-start.3) | collective-permute-done | bytes 131104 | tf_op jit(solution)/shard_map/ppermute | solution.py:25
  42.7 3.4 %collective-permute-start.4 = (bf16[2,2,2,64,256]{4,3,0,1,2:T(8,128)(2,1)S(1)}, bf16[2,2,2,64,256]{4,3,0,1,2:T(8,128)(2,1)S(1)}, u32[]{:S(2)}, u32[]{:S(2)}) collective-permute-start(bf16[2,2,2,64,256]{4,3,0,1,2:T(8,128)(2,1)S(1)} %maximum_select_fusion.6), channel_id=1, source_target_pairs={{0,16},{4,20},{8,24},{12,28},{16,0},{20,4},{24,8},{28,12},{32,48},... | collective-permute-start | bytes 786440 | tf_op jit(solution)/shard_map/ppermute | solution.py:25
  46.3 11.2 %collective-permute-done.4 = bf16[2,2,2,64,256]{4,3,0,1,2:T(8,128)(2,1)S(1)} collective-permute-done((bf16[2,2,2,64,256]{4,3,0,1,2:T(8,128)(2,1)S(1)}, bf16[2,2,2,64,256]{4,3,0,1,2:T(8,128)(2,1)S(1)}, u32[]{:S(2)}, u32[]{:S(2)}) %collective-permute-start.4) | collective-permute-done | bytes 262176 | tf_op jit(solution)/shard_map/ppermute | solution.py:25
  57.6 1.1 fusion.89
  58.7 0.7 copy.123
  59.5 0.7 copy.124
  60.3 11.2 %collective-permute-done.5 = bf16[2,2,2,2,64,256]{5,4,0,1,2,3:T(8,128)(2,1)S(1)} collective-permute-done((bf16[2,2,2,2,64,256]{5,4,0,1,2,3:T(8,128)(2,1)S(1)}, bf16[2,2,2,2,64,256]{5,4,0,1,2,3:T(8,128)(2,1)S(1)}, u32[]{:S(2)}, u32[]{:S(2)}) %collective-permute-start.5) | collective-permute-done | bytes 524320 | tf_op jit(solution)/shard_map/ppermute | solution.py:25
  72.9 1.5 collective-permute-done.6
  74.6 25.0 %all-gather.2.cloned.1.call-done = bf16[4096,768]{1,0:T(8,128)(2,1)} async-done(((bf16[64,768]{1,0:T(8,128)(2,1)}), bf16[4096,768]{1,0:T(8,128)(2,1)}) %all-gather.2.cloned.1.call-update) | async-done | bytes 6291472 | tf_op jit(solution)/shard_map/all_gather | solution.py:133
  99.6 3.9 %convolution_convert_fusion.1 = bf16[128,768]{1,0:T(8,128)(2,1)S(1)} fusion(bf16[4096,768]{1,0:T(8,128)(2,1)} %all-gather.2.cloned.1.call-done, bf16[128,4096]{1,0:T(8,128)(2,1)S(1)} %copy-done, f32[4096]{0:T(1024)S(1)} %copy-done.17, f32[128]{0:T(128)S(1)} %get-tuple-element.53), kind=kOutput, calls=%fused_computation.26 | convolution fusion | flops 807501824 | bytes 7553536 | tf_op jit(solution)/shard_map/dot_general | solution.py:137
  103.6 0.6 slice.144
  104.1 2.1 collective-permute-start
  106.3 1.1 convolution_bitcast_fusion.3
  107.8 3.6 %collective-permute-done = bf16[2,3,256]{2,0,1:T(2,128)(2,1)S(1)} collective-permute-done((bf16[2,3,256]{2,0,1:T(2,128)(2,1)}, bf16[2,3,256]{2,0,1:T(2,128)(2,1)S(1)}, u32[]{:S(2)}, u32[]{:S(2)}) %collective-permute-start) | collective-permute-done | bytes 3104 | tf_op jit(solution)/shard_map/ppermute | solution.py:14
  111.6 0.7 maximum_bitcast_fusion.2
  112.3 1.8 copy.120
  114.1 6.5 %all-to-all-start = ((f32[2,256,128]{2,0,1:T(2,128)}), f32[2,256,128]{2,0,1:T(2,128)}, u32[]{:S(2)}, u32[]{:S(2)}) async-start(f32[2,256,128]{2,0,1:T(2,128)} %copy.120), calls=%async_computation | async-start | bytes 524288 | tf_op jit(solution)/shard_map/all_to_all | solution.py:52
  120.6 0.9 fusion.81
  121.6 0.6 copy-done.11
  122.2 1.3 convolution_bitcast_fusion.2
  123.5 0.9 multiply_add_fusion.5
  124.4 2.3 convolution_bitcast_fusion.1
  126.8 5.3 %all-to-all-done = f32[2,256,128]{2,0,1:T(2,128)} async-done(((f32[2,256,128]{2,0,1:T(2,128)}), f32[2,256,128]{2,0,1:T(2,128)}, u32[]{:S(2)}, u32[]{:S(2)}) %all-to-all-start) | async-done | bytes 262176 | tf_op jit(solution)/shard_map/all_to_all | solution.py:52
  132.1 1.6 convolution_bitcast_fusion
  133.7 1.0 multiply_add_fusion.1
  134.8 1.0 fusion.19
  136.0 0.8 fusion
  137.7 0.6 fusion.16
  138.3 1.0 copy.131
  139.3 6.6 %all-to-all-start.2 = ((f32[64,3,4,128]{3,2,1,0:T(4,128)}), f32[64,3,4,128]{3,2,1,0:T(4,128)}, u32[]{:S(2)}, u32[]{:S(2)}) async-start(f32[64,3,4,128]{3,2,1,0:T(4,128)} %copy.131), calls=%async_computation.2 | async-start | bytes 786432 | tf_op jit(solution)/shard_map/all_to_all | solution.py:60
  146.0 0.6 pad.17.clone
  146.6 13.4 %all-to-all-done.2 = f32[64,3,4,128]{3,2,1,0:T(4,128)} async-done(((f32[64,3,4,128]{3,2,1,0:T(4,128)}), f32[64,3,4,128]{3,2,1,0:T(4,128)}, u32[]{:S(2)}, u32[]{:S(2)}) %all-to-all-start.2) | async-done | bytes 393248 | tf_op jit(solution)/shard_map/all_to_all | solution.py:60
  160.0 1.8 slice_multiply_fusion.6
  161.7 1.7 copy.132
  163.4 1.7 copy.134
  165.1 1.7 copy.135
  166.7 1.1 fusion.55
  167.9 2.9 %collective-permute-start.7 = (f32[2,3,256]{2,0,1:T(2,128)S(1)}, f32[2,3,256]{2,0,1:T(2,128)S(1)}, u32[]{:S(2)}, u32[]{:S(2)}) collective-permute-start(f32[2,3,256]{2,0,1:T(2,128)S(1)} %slice.165), channel_id=1, source_target_pairs={{4,0},{8,4},{12,8},{16,12},{20,16},{24,20},{28,24},{32,28},{36,32}... | collective-permute-start | bytes 18440 | tf_op jit(solution)/shard_map/ppermute | solution.py:14
  170.8 0.8 convolution_convert_fusion
  172.5 5.0 %fusion.90 = (bf16[128,4096]{1,0:T(8,128)(2,1)S(1)}, f32[128]{0:T(128)S(1)}) fusion(bf16[128,4096]{1,0:T(8,128)(2,1)S(1)} %copy-done, f32[4096]{0:T(1024)S(1)} %copy-done.18, bf16[128,768]{0,1:T(8,128)(2,1)S(1)} %bitcast.206, bf16[4096,768]{1,0:T(8,128)(2,1)} %all-gather.2.cloned.1.call-done), kind=kOutput, calls=%fused_computation.176 | convolution fusion | flops 807927680 | bytes 8602112 | tf_op jit(solution)/shard_map/dot_general | solution.py:184
  177.5 1.3 copy.137
  178.8 1.5 copy.138
  180.7 1.6 pad_maximum_fusion
  182.6 32.0 %reduce-scatter.2.cloned.1.call-done = bf16[1,128,2176]{2,1,0:T(8,128)(2,1)} async-done(((bf16[4,128,2176]{2,1,0:T(8,128)(2,1)}), bf16[1,128,2176]{2,1,0:T(8,128)(2,1)}) %reduce-scatter.2.cloned.1.call-update) | async-done | bytes 557072 | tf_op jit(solution)/shard_map/reduce_scatter | solution.py:205
  214.6 1.1 bitcast_convert_fusion
  216.0 1.9 fusion.29
  217.9 1.4 collective-permute-start.8
  219.3 8.0 %collective-permute-done.8 = bf16[1,128,1024]{2,1,0:T(8,128)(2,1)S(1)} collective-permute-done((bf16[1,128,1024]{2,1,0:T(8,128)(2,1)S(1)}, bf16[1,128,1024]{2,1,0:T(8,128)(2,1)S(1)}, u32[]{:S(2)}, u32[]{:S(2)}) %collective-permute-start.8) | collective-permute-done | bytes 262176 | tf_op jit(solution)/shard_map/ppermute | solution.py:25
  227.8 0.8 copy.144
  228.6 11.7 %collective-permute-done.9 = bf16[2,1,128,1024]{3,2,1,0:T(8,128)(2,1)S(1)} collective-permute-done((bf16[2,1,128,1024]{3,2,1,0:T(8,128)(2,1)S(1)}, bf16[2,1,128,1024]{3,2,1,0:T(8,128)(2,1)S(1)}, u32[]{:S(2)}, u32[]{:S(2)}) %collective-permute-start.9) | collective-permute-done | bytes 524320 | tf_op jit(solution)/shard_map/ppermute | solution.py:25
  240.6 0.7 copy.142
  241.2 1.3 copy.143
  (105 shorter events, 6.0 us)
Async XLA Ops:
  7.2 92.5 %all-gather.2.cloned.1.call-start = ((), (), s32[]{:S(2)}) async-start(), calls=%async_computation.4 | async-start | bytes 6389760 | tf_op jit(solution)/shard_map/all_gather | solution.py:133
  8.8 16.6 %collective-permute-start.1 = (bf16[64,256]{1,0:T(8,128)(2,1)}, bf16[64,256]{1,0:T(8,128)(2,1)S(1)}, u32[]{:S(2)}, u32[]{:S(2)}) collective-permute-start(bf16[64,256]{1,0:T(8,128)(2,1)} %bitcast.213), channel_id=1, source_target_pairs={{0,128},{4,132},{8,136},{12,140},{16,144},{20,148},{24,152},{28,15... | collective-permute-start | bytes 98312 | tf_op jit(solution)/shard_map/ppermute | solution.py:25
  12.6 101.5 %all-to-all-start.1 = ((f32[1,256,128]{2,0,1:T(1,128)}), f32[1,256,128]{2,0,1:T(1,128)}, u32[]{:S(2)}, u32[]{:S(2)}) async-start(f32[1,256,128]{2,0,1:T(1,128)} %bitcast.1), calls=%async_computation.1 | async-start | bytes 262144 | tf_op jit(solution)/shard_map/all_to_all | solution.py:52
  26.2 4.8 %collective-permute-start.2 = (bf16[2,64,256]{2,1,0:T(8,128)(2,1)S(1)}, bf16[2,64,256]{2,1,0:T(8,128)(2,1)S(1)}, u32[]{:S(2)}, u32[]{:S(2)}) collective-permute-start(bf16[2,64,256]{2,1,0:T(8,128)(2,1)S(1)} %maximum_select_fusion.8), channel_id=1, source_target_pairs={{0,64},{4,68},{8,72},{12,76},{16,80},{20,84},{24,88},{28,92},{32,9... | collective-permute-start | bytes 196616 | tf_op jit(solution)/shard_map/ppermute | solution.py:25
  31.0 11.7 %collective-permute-start.3 = (bf16[2,2,64,256]{3,2,0,1:T(8,128)(2,1)S(1)}, bf16[2,2,64,256]{3,2,0,1:T(8,128)(2,1)S(1)}, u32[]{:S(2)}, u32[]{:S(2)}) collective-permute-start(bf16[2,2,64,256]{3,2,0,1:T(8,128)(2,1)S(1)} %maximum_select_fusion.7), channel_id=1, source_target_pairs={{0,32},{4,36},{8,40},{12,44},{16,48},{20,52},{24,56},{28,60},{32,0... | collective-permute-start | bytes 393224 | tf_op jit(solution)/shard_map/ppermute | solution.py:25
  42.7 14.7 %collective-permute-start.4 = (bf16[2,2,2,64,256]{4,3,0,1,2:T(8,128)(2,1)S(1)}, bf16[2,2,2,64,256]{4,3,0,1,2:T(8,128)(2,1)S(1)}, u32[]{:S(2)}, u32[]{:S(2)}) collective-permute-start(bf16[2,2,2,64,256]{4,3,0,1,2:T(8,128)(2,1)S(1)} %maximum_select_fusion.6), channel_id=1, source_target_pairs={{0,16},{4,20},{8,24},{12,28},{16,0},{20,4},{24,8},{28,12},{32,48},... | collective-permute-start | bytes 786440 | tf_op jit(solution)/shard_map/ppermute | solution.py:25
  57.5 14.0 %collective-permute-start.5 = (bf16[2,2,2,2,64,256]{5,4,0,1,2,3:T(8,128)(2,1)S(1)}, bf16[2,2,2,2,64,256]{5,4,0,1,2,3:T(8,128)(2,1)S(1)}, u32[]{:S(2)}, u32[]{:S(2)}) collective-permute-start(bf16[2,2,2,2,64,256]{5,4,0,1,2,3:T(8,128)(2,1)S(1)} %maximum_select_fusion.3), channel_id=1, source_target_pairs={{0,8},{4,12},{8,0},{12,4},{16,24},{20,28},{24,16},{28,20},{32,40},... | collective-permute-start | bytes 1572872 | tf_op jit(solution)/shard_map/ppermute | solution.py:25
  58.7 1.4 copy-start.7
  58.7 1.4 copy-start.9
  60.3 11.5 %copy-start = (bf16[128,4096]{1,0:T(8,128)(2,1)S(1)}, bf16[128,4096]{1,0:T(8,128)(2,1)}, u32[]{:S(2)}) copy-start(bf16[128,4096]{1,0:T(8,128)(2,1)} %param.8) | copy-start | bytes 3145732
  71.7 2.8 %collective-permute-start.6 = (bf16[2,2,2,2,2,64,256]{6,5,0,1,2,3,4:T(8,128)(2,1)S(1)}, bf16[2,2,2,2,2,64,256]{6,5,0,1,2,3,4:T(8,128)(2,1)S(1)}, u32[]{:S(2)}, u32[]{:S(2)}) collective-permute-start(bf16[2,2,2,2,2,64,256]{6,5,0,1,2,3,4:T(8,128)(2,1)S(1)} %maximum_select_fusion.1), channel_id=1, source_target_pairs={{0,4},{4,0},{8,12},{12,8},{16,20},{20,16},{24,28},{28,24},{32,36},... | collective-permute-start | bytes 3145736 | tf_op jit(solution)/shard_map/ppermute | solution.py:25
  72.6 27.0 %copy-start.22 = (f32[128]{0:T(128)}, f32[128]{0:T(128)S(1)}, u32[]{:S(2)}) copy-start(f32[128]{0:T(128)S(1)} %get-tuple-element.53) | copy-start | bytes 1540
  74.4 25.2 %copy-start.17 = (f32[4096]{0:T(1024)S(1)}, f32[4096]{0:T(1024)}, u32[]{:S(2)}) copy-start(f32[4096]{0:T(1024)} %param.9) | copy-start | bytes 49156
  99.6 6.6 %copy-start.2 = (bf16[128,4096]{1,0:T(8,128)(2,1)S(1)}, bf16[128,4096]{1,0:T(8,128)(2,1)}, u32[]{:S(2)}) copy-start(bf16[128,4096]{1,0:T(8,128)(2,1)} %param.15) | copy-start | bytes 3145732
  104.1 7.2 %collective-permute-start = (bf16[2,3,256]{2,0,1:T(2,128)(2,1)}, bf16[2,3,256]{2,0,1:T(2,128)(2,1)S(1)}, u32[]{:S(2)}, u32[]{:S(2)}) collective-permute-start(bf16[2,3,256]{2,0,1:T(2,128)(2,1)} %bitcast.6), channel_id=1, source_target_pairs={{0,4},{4,8},{8,12},{12,16},{16,20},{20,24},{24,28},{28,32},{32,36}... | collective-permute-start | bytes 9224 | tf_op jit(solution)/shard_map/ppermute | solution.py:14
  107.7 3.8 %copy-start.3 = (f32[128,256]{1,0:T(8,128)S(1)}, f32[128,256]{1,0:T(8,128)}, u32[]{:S(2)}) copy-start(f32[128,256]{1,0:T(8,128)} %convolution_bitcast_fusion.3) | copy-start | bytes 393220
  114.1 17.9 %all-to-all-start = ((f32[2,256,128]{2,0,1:T(2,128)}), f32[2,256,128]{2,0,1:T(2,128)}, u32[]{:S(2)}, u32[]{:S(2)}) async-start(f32[2,256,128]{2,0,1:T(2,128)} %copy.120), calls=%async_computation | async-start | bytes 524288 | tf_op jit(solution)/shard_map/all_to_all | solution.py:52
  121.5 0.6 copy-start.11
  121.5 0.6 copy-start.13
  132.1 2.7 %copy-start.4 = (f32[128,128]{1,0:T(8,128)S(1)}, f32[128,128]{1,0:T(8,128)}, u32[]{:S(2)}) copy-start(f32[128,128]{1,0:T(8,128)} %get-tuple-element.42) | copy-start | bytes 196612
  132.1 2.7 %copy-start.5 = (f32[128,128]{1,0:T(8,128)S(1)}, f32[128,128]{1,0:T(8,128)}, u32[]{:S(2)}) copy-start(f32[128,128]{1,0:T(8,128)} %get-tuple-element.44) | copy-start | bytes 196612
  132.1 2.7 %copy-start.6 = (f32[128,128]{1,0:T(8,128)S(1)}, f32[128,128]{1,0:T(8,128)}, u32[]{:S(2)}) copy-start(f32[128,128]{1,0:T(8,128)} %get-tuple-element.46) | copy-start | bytes 196612
  134.7 1.1 copy-start.1
  136.0 0.9 copy-start.8
  136.0 0.9 copy-start.10
  136.9 0.8 copy-start.12
  136.9 0.8 copy-start.14
  137.6 29.1 %copy-start.19 = (f32[256]{0:T(256)S(1)}, f32[256]{0:T(256)}, u32[]{:S(2)}) copy-start(f32[256]{0:T(256)} %param.13) | copy-start | bytes 3076
  139.3 20.7 %all-to-all-start.2 = ((f32[64,3,4,128]{3,2,1,0:T(4,128)}), f32[64,3,4,128]{3,2,1,0:T(4,128)}, u32[]{:S(2)}, u32[]{:S(2)}) async-start(f32[64,3,4,128]{3,2,1,0:T(4,128)} %copy.131), calls=%async_computation.2 | async-start | bytes 786432 | tf_op jit(solution)/shard_map/all_to_all | solution.py:60
  145.9 68.7 %reduce-scatter.2.cloned.1.call-start = ((), (), s32[]{:S(2)}) async-start(), calls=%async_computation.5 | async-start | bytes 2785280 | tf_op jit(solution)/shard_map/reduce_scatter | solution.py:205
  166.7 4.1 %copy-start.15 = (f32[128,1,256]{2,0,1:T(8,128)S(1)}, f32[128,1,256]{2,0,1:T(8,128)}, u32[]{:S(2)}) copy-start(f32[128,1,256]{2,0,1:T(8,128)} %copy.132) | copy-start | bytes 393220
  167.9 4.2 %collective-permute-start.7 = (f32[2,3,256]{2,0,1:T(2,128)S(1)}, f32[2,3,256]{2,0,1:T(2,128)S(1)}, u32[]{:S(2)}, u32[]{:S(2)}) collective-permute-start(f32[2,3,256]{2,0,1:T(2,128)S(1)} %slice.165), channel_id=1, source_target_pairs={{4,0},{8,4},{12,8},{16,12},{20,16},{24,20},{28,24},{32,28},{36,32}... | collective-permute-start | bytes 18440 | tf_op jit(solution)/shard_map/ppermute | solution.py:14
  171.6 0.8 copy-start.18
  177.5 3.1 %copy-start.20 = (bf16[128]{0:T(256)(128)(2,1)S(1)}, bf16[128]{0:T(256)(128)(2,1)}, u32[]{:S(2)}) copy-start(bf16[128]{0:T(256)(128)(2,1)} %pad.17.clone) | copy-start | bytes 772
  182.3 33.6 %copy-start.21 = (f32[128]{0:T(128)S(1)}, f32[128]{0:T(128)}, u32[]{:S(2)}) copy-start(f32[128]{0:T(128)} %get-tuple-element.52) | copy-start | bytes 1540
  182.4 33.6 %copy-start.23 = (f32[128]{0:T(128)S(1)}, f32[128]{0:T(128)}, u32[]{:S(2)}) copy-start(f32[128]{0:T(128)} %copy-done.22) | copy-start | bytes 1540
  215.8 12.0 %copy-start.16 = (f32[1,128,64,4]{1,3,0,2:T(4,128)S(1)}, f32[1,128,64,4]{1,3,0,2:T(4,128)}, u32[]{:S(2)}) copy-start(f32[1,128,64,4]{1,3,0,2:T(4,128)} %get-tuple-element.35) | copy-start | bytes 393220
  217.9 9.5 %collective-permute-start.8 = (bf16[1,128,1024]{2,1,0:T(8,128)(2,1)S(1)}, bf16[1,128,1024]{2,1,0:T(8,128)(2,1)S(1)}, u32[]{:S(2)}, u32[]{:S(2)}) collective-permute-start(bf16[1,128,1024]{2,1,0:T(8,128)(2,1)S(1)} %bitcast.192), channel_id=1, source_target_pairs={{0,2},{1,3},{2,0},{3,1},{4,6},{5,7},{6,4},{7,5},{8,10},{9,11},{10,... | collective-permute-start | bytes 786440 | tf_op jit(solution)/shard_map/ppermute | solution.py:25
  227.5 12.8 %collective-permute-start.9 = (bf16[2,1,128,1024]{3,2,1,0:T(8,128)(2,1)S(1)}, bf16[2,1,128,1024]{3,2,1,0:T(8,128)(2,1)S(1)}, u32[]{:S(2)}, u32[]{:S(2)}) collective-permute-start(bf16[2,1,128,1024]{3,2,1,0:T(8,128)(2,1)S(1)} %maximum_select_fusion.5), channel_id=1, source_target_pairs={{0,1},{1,0},{2,3},{3,2},{4,5},{5,4},{6,7},{7,6},{8,9},{9,8},{10,11... | collective-permute-start | bytes 1572872 | tf_op jit(solution)/shard_map/ppermute | solution.py:25
Sparse Core Ops, SparseCore 0:
  11.3 88.2 all-gather.1
  182.5 32.1 reduce-scatter.1
where the time goes:
time: 251 us; the launch traced here: 249 us
  waiting for transfers between devices  132 us (53%)
  starting transfers between devices  42.9 us (17%)
  local copies, waits for them, and re-layouts  22.1 us (9%)
  other arithmetic  18.8 us (7%)
  matrix products  18.6 us (7%)
  between operations  14.7 us (6%)
    ppermute x8, waiting for transfers between devices, doubled_gather(): arrived = lax.ppermute(gathered, axis, route)  52.5 us
    reduce_scatter x1, waiting for transfers between devices, per_device(): lax.psum_scatter(payload, 'ch', scatter_dimension=0).astype(jnp.float32)  32 us
    all_gather x1, waiting for transfers between devices, per_device(): lax.all_gather(in_weight.reshape(in_weight.shape[0], -1), 'seq', axis=0,...  25 us
    all_to_all x2, starting transfers between devices, to_columns(): lax.all_to_all(signals, 'seq', split_axis=1, concat_axis=2, tiled=True)  17.7 us
    ppermute x8, starting transfers between devices, doubled_gather(): arrived = lax.ppermute(gathered, axis, route)  13.5 us
    all_to_all x1, waiting for transfers between devices, to_rows(): lax.all_to_all(pieces, 'seq', split_axis=0, concat_axis=0, tiled=True)  13.4 us
    all_to_all x1, starting transfers between devices, to_rows(): lax.all_to_all(pieces, 'seq', split_axis=0, concat_axis=0, tiled=True)  6.64 us
    all_to_all x2, waiting for transfers between devices, to_columns(): lax.all_to_all(signals, 'seq', split_axis=1, concat_axis=2, tiled=True)  5.28 us
  transfers between devices with their start and end apart: 15, of which 13 were waited for; matrix products, arithmetic and copies ran while one was open for 11% of the time, Pallas kernels for 0%

commit v1 on v0

--- a/solution.py
+++ b/solution.py
@@ -130,7 +130,15 @@
     inv_rms = lax.rsqrt(jnp.mean(wide_inputs * wide_inputs, axis=1, keepdims=True) + epsilon)
     normed = (wide_inputs * inv_rms * norm_gain).astype(jnp.bfloat16)
     in_panel, out_panel = (
-        lax.all_gather(in_weight.reshape(in_weight.shape[0], -1), "seq", axis=0, tiled=True),
+        jnp.concatenate(
+            lax.all_to_all(
+                jnp.stack([in_weight.reshape(in_weight.shape[0], -1)] * lax.axis_size("seq")),
+                "seq",
+                0,
+                0,
+            ),
+            axis=0,
+        ),
         doubled_gather(out_weight.T, "seq").T,
     )
     in_flat = in_panel.reshape(model_width, 3 * slab_width)

time: 251 us -> 364 us (1.45)
  waiting for transfers between devices: 132 us -> 235 us
  starting transfers between devices: 42.9 us -> 51.6 us
    ppermute x8, waiting for transfers between devices: 52.5 us -> 181 us  [doubled_gather(): arrived = lax.ppermute(gathered, axis, route)]
    all_gather x1 -> x0, waiting for transfers between devices: 25 us -> none  [per_device(): lax.all_gather(in_weight.reshape(in_weight.shape[0], -1), 'seq', axis=0,...]
    all_to_all x0 -> x1, starting transfers between devices: none -> 12.3 us  [per_device(): lax.all_to_all(jnp.stack([in_weight.reshape(in_weight.shape[0], -1)] * la...]
    ppermute x8, starting transfers between devices: 13.5 us -> 8.18 us  [doubled_gather(): arrived = lax.ppermute(gathered, axis, route)]
    another operation x0 -> x2, local copies, waits for them, and re-layouts: none -> 4.34 us  [per_device(): jnp.stack([in_weight.reshape(in_weight.shape[0], -1)] * lax.axis_size('se...]
  transfers between devices with their start and end apart: 15 -> 15, of which waited for: 13 -> 12; matrix products, arithmetic and copies ran while one was open for 11% -> 7% of each run, Pallas kernels for 0% -> 0%
where the time goes in v1:
time: 364 us; the launch traced here: 363 us
  waiting for transfers between devices  235 us (65%)
  starting transfers between devices  51.6 us (14%)
  local copies, waits for them, and re-layouts  24.5 us (7%)
  matrix products  19.6 us (5%)
  other arithmetic  16.9 us (5%)
  between operations  14.8 us (4%)
    ppermute x8, waiting for transfers between devices, doubled_gather(): arrived = lax.ppermute(gathered, axis, route)  181 us
    reduce_scatter x1, waiting for transfers between devices, per_device(): lax.psum_scatter(payload, 'ch', scatter_dimension=0).astype(jnp.float32)  31.8 us
    all_to_all x2, starting transfers between devices, to_columns(): lax.all_to_all(signals, 'seq', split_axis=1, concat_axis=2, tiled=True)  19.6 us
    all_to_all x1, waiting for transfers between devices, to_rows(): lax.all_to_all(pieces, 'seq', split_axis=0, concat_axis=0, tiled=True)  13.3 us
    all_to_all x1, starting transfers between devices, per_device(): lax.all_to_all(jnp.stack([in_weight.reshape(in_weight.shape[0], -1)] * la...  12.3 us
    ppermute x8, starting transfers between devices, doubled_gather(): arrived = lax.ppermute(gathered, axis, route)  8.18 us
  transfers between devices with their start and end apart: 15, of which 12 were waited for; matrix products, arithmetic and copies ran while one was open for 7% of the time, Pallas kernels for 0%

profile of v1, /device:TPU:2, one launch (start us, length us, event | category | flops | bytes accessed | tf_op | source)
XLA Modules:
  0.0 362.6 jit_solution(17371574400792910458)
XLA Ops:
  7.2 0.9 copy.156
  8.1 3.4 stack.178
  11.5 12.3 %all-to-all-start = ((bf16[64,64,768]{2,1,0:T(8,128)(2,1)}), bf16[64,64,768]{2,1,0:T(8,128)(2,1)}, u32[]{:S(2)}, u32[]{:S(2)}) async-start(bf16[64,64,768]{2,1,0:T(8,128)(2,1)} %stack.178), calls=%async_computation | async-start | bytes 12582912 | tf_op jit(solution)/shard_map/all_to_all | solution.py:134
  23.9 2.4 collective-permute-start.1
  26.2 0.6 iota_multiply_fusion.1
  26.9 14.4 %collective-permute-done.1 = bf16[64,256]{1,0:T(8,128)(2,1)S(1)} collective-permute-done((bf16[64,256]{1,0:T(8,128)(2,1)S(1)}, bf16[64,256]{1,0:T(8,128)(2,1)S(1)}, u32[]{:S(2)}, u32[]{:S(2)}) %collective-permute-start.1) | collective-permute-done | bytes 32800 | tf_op jit(solution)/shard_map/ppermute | solution.py:25
  41.9 4.3 %collective-permute-done.2 = bf16[2,64,256]{2,1,0:T(8,128)(2,1)S(1)} collective-permute-done((bf16[2,64,256]{2,1,0:T(8,128)(2,1)S(1)}, bf16[2,64,256]{2,1,0:T(8,128)(2,1)S(1)}, u32[]{:S(2)}, u32[]{:S(2)}) %collective-permute-start.2) | collective-permute-done | bytes 65568 | tf_op jit(solution)/shard_map/ppermute | solution.py:25
  46.2 2.6 collective-permute-start.3
  48.8 121.6 %collective-permute-done.3 = bf16[2,2,64,256]{3,2,0,1:T(8,128)(2,1)S(1)} collective-permute-done((bf16[2,2,64,256]{3,2,0,1:T(8,128)(2,1)S(1)}, bf16[2,2,64,256]{3,2,0,1:T(8,128)(2,1)S(1)}, u32[]{:S(2)}, u32[]{:S(2)}) %collective-permute-start.3) | collective-permute-done | bytes 131104 | tf_op jit(solution)/shard_map/ppermute | solution.py:25
  170.4 0.7 collective-permute-start.4
  171.3 11.5 %collective-permute-done.4 = bf16[2,2,2,64,256]{4,3,0,1,2:T(8,128)(2,1)S(1)} collective-permute-done((bf16[2,2,2,64,256]{4,3,0,1,2:T(8,128)(2,1)S(1)}, bf16[2,2,2,64,256]{4,3,0,1,2:T(8,128)(2,1)S(1)}, u32[]{:S(2)}, u32[]{:S(2)}) %collective-permute-start.4) | collective-permute-done | bytes 262176 | tf_op jit(solution)/shard_map/ppermute | solution.py:25
  182.9 1.1 fusion.89
  184.0 0.7 copy.124
  184.7 0.7 copy.123
  185.4 0.8 copy.126
  186.4 8.1 %collective-permute-done.5 = bf16[2,2,2,2,64,256]{5,4,0,1,2,3:T(8,128)(2,1)S(1)} collective-permute-done((bf16[2,2,2,2,64,256]{5,4,0,1,2,3:T(8,128)(2,1)S(1)}, bf16[2,2,2,2,64,256]{5,4,0,1,2,3:T(8,128)(2,1)S(1)}, u32[]{:S(2)}, u32[]{:S(2)}) %collective-permute-start.5) | collective-permute-done | bytes 524320 | tf_op jit(solution)/shard_map/ppermute | solution.py:25
  195.8 1.5 collective-permute-done.6
  197.5 9.9 %all-to-all-start.2 = ((f32[1,256,128]{2,0,1:T(1,128)}), f32[1,256,128]{2,0,1:T(1,128)}, u32[]{:S(2)}, u32[]{:S(2)}) async-start(f32[1,256,128]{2,0,1:T(1,128)} %bitcast.1), calls=%async_computation.2 | async-start | bytes 262144 | tf_op jit(solution)/shard_map/all_to_all | solution.py:52
  207.5 3.9 %convolution_convert_fusion.1 = bf16[128,768]{1,0:T(8,128)(2,1)S(1)} fusion(bf16[4096,768]{1,0:T(8,128)(2,1)} %bitcast.6, bf16[128,4096]{1,0:T(8,128)(2,1)S(1)} %copy-done, f32[4096]{0:T(1024)S(1)} %copy-done.24, f32[128]{0:T(128)S(1)} %get-tuple-element.53), kind=kOutput, calls=%fused_computation.26 | convolution fusion | flops 807501824 | bytes 7553536 | tf_op jit(solution)/shard_map/dot_general | solution.py:145
  211.4 0.6 slice.144
  212.0 2.0 collective-permute-start
  214.0 1.1 convolution_bitcast_fusion.3
  215.5 3.7 %collective-permute-done = bf16[2,3,256]{2,0,1:T(2,128)(2,1)S(1)} collective-permute-done((bf16[2,3,256]{2,0,1:T(2,128)(2,1)}, bf16[2,3,256]{2,0,1:T(2,128)(2,1)S(1)}, u32[]{:S(2)}, u32[]{:S(2)}) %collective-permute-start) | collective-permute-done | bytes 3104 | tf_op jit(solution)/shard_map/ppermute | solution.py:14
  219.4 0.7 maximum_bitcast_fusion.2
  220.2 1.8 copy.120
  221.9 9.6 %all-to-all-start.1 = ((f32[2,256,128]{2,0,1:T(2,128)}), f32[2,256,128]{2,0,1:T(2,128)}, u32[]{:S(2)}, u32[]{:S(2)}) async-start(f32[2,256,128]{2,0,1:T(2,128)} %copy.120), calls=%async_computation.1 | async-start | bytes 524288 | tf_op jit(solution)/shard_map/all_to_all | solution.py:52
  231.6 0.9 fusion.81
  232.5 0.6 copy-done.17
  233.1 1.3 convolution_bitcast_fusion.2
  234.4 0.9 multiply_add_fusion.5
  235.4 2.3 convolution_bitcast_fusion.1
  237.7 5.3 %all-to-all-done.1 = f32[2,256,128]{2,0,1:T(2,128)} async-done(((f32[2,256,128]{2,0,1:T(2,128)}), f32[2,256,128]{2,0,1:T(2,128)}, u32[]{:S(2)}, u32[]{:S(2)}) %all-to-all-start.1) | async-done | bytes 262176 | tf_op jit(solution)/shard_map/all_to_all | solution.py:52
  243.0 1.6 convolution_bitcast_fusion
  244.7 1.0 multiply_add_fusion.1
  245.7 1.0 fusion.19
  247.0 0.8 fusion
  248.6 0.6 fusion.16
  249.2 1.0 copy.131
  250.2 6.6 %all-to-all-start.3 = ((f32[64,3,4,128]{3,2,1,0:T(4,128)}), f32[64,3,4,128]{3,2,1,0:T(4,128)}, u32[]{:S(2)}, u32[]{:S(2)}) async-start(f32[64,3,4,128]{3,2,1,0:T(4,128)} %copy.131), calls=%async_computation.3 | async-start | bytes 786432 | tf_op jit(solution)/shard_map/all_to_all | solution.py:60
  257.0 0.7 pad.17.clone
  257.6 13.3 %all-to-all-done.3 = f32[64,3,4,128]{3,2,1,0:T(4,128)} async-done(((f32[64,3,4,128]{3,2,1,0:T(4,128)}), f32[64,3,4,128]{3,2,1,0:T(4,128)}, u32[]{:S(2)}, u32[]{:S(2)}) %all-to-all-start.3) | async-done | bytes 393248 | tf_op jit(solution)/shard_map/all_to_all | solution.py:60
  270.9 1.8 slice_multiply_fusion.6
  272.7 1.7 copy.135
  274.4 1.7 copy.134
  276.0 1.1 fusion.55
  277.2 0.7 copy-done.2
  277.9 0.6 slice.165
  278.5 2.8 collective-permute-start.7
  281.3 1.7 copy.132
  283.0 1.8 convolution_convert_fusion
  284.9 0.7 pad_maximum_fusion.5
  286.0 5.0 %fusion.90 = (bf16[128,4096]{1,0:T(8,128)(2,1)S(1)}, f32[128]{0:T(128)S(1)}) fusion(bf16[128,4096]{1,0:T(8,128)(2,1)S(1)} %copy-done, f32[4096]{0:T(1024)S(1)} %copy-done.25, bf16[128,768]{0,1:T(8,128)(2,1)S(1)} %bitcast.207, bf16[4096,768]{1,0:T(8,128)(2,1)} %bitcast.6), kind=kOutput, calls=%fused_computation.176 | convolution fusion | flops 807927680 | bytes 8602112 | tf_op jit(solution)/shard_map/dot_general | solution.py:192
  291.3 1.3 copy.137
  292.6 1.5 copy.138
  294.2 1.6 pad_maximum_fusion
  296.1 31.8 %reduce-scatter.2.cloned.1.call-done = bf16[1,128,2176]{2,1,0:T(8,128)(2,1)} async-done(((bf16[4,128,2176]{2,1,0:T(8,128)(2,1)}), bf16[1,128,2176]{2,1,0:T(8,128)(2,1)}) %reduce-scatter.2.cloned.1.call-update) | async-done | bytes 557072 | tf_op jit(solution)/shard_map/reduce_scatter | solution.py:213
  327.9 1.1 bitcast_convert_fusion
  329.2 1.9 fusion.29
  331.1 1.5 collective-permute-start.8
  332.6 8.0 %collective-permute-done.8 = bf16[1,128,1024]{2,1,0:T(8,128)(2,1)S(1)} collective-permute-done((bf16[1,128,1024]{2,1,0:T(8,128)(2,1)S(1)}, bf16[1,128,1024]{2,1,0:T(8,128)(2,1)S(1)}, u32[]{:S(2)}, u32[]{:S(2)}) %collective-permute-start.8) | collective-permute-done | bytes 262176 | tf_op jit(solution)/shard_map/ppermute | solution.py:25
  341.0 0.8 copy.144
  341.8 11.7 %collective-permute-done.9 = bf16[2,1,128,1024]{3,2,1,0:T(8,128)(2,1)S(1)} collective-permute-done((bf16[2,1,128,1024]{3,2,1,0:T(8,128)(2,1)S(1)}, bf16[2,1,128,1024]{3,2,1,0:T(8,128)(2,1)S(1)}, u32[]{:S(2)}, u32[]{:S(2)}) %collective-permute-start.9) | collective-permute-done | bytes 524320 | tf_op jit(solution)/shard_map/ppermute | solution.py:25
  353.8 0.7 copy.142
  354.4 1.3 copy.143
  (121 shorter events, 6.1 us)
Async XLA Ops:
  11.5 12.3 %copy-start.22 = (bf16[256,64]{0,1:T(8,128)(2,1)S(1)}, bf16[256,64]{0,1:T(8,128)(2,1)}, u32[]{:S(2)}) copy-start(bf16[256,64]{0,1:T(8,128)(2,1)} %param.14) | copy-start | bytes 98308
  11.5 14.7 %copy-start.26 = (f32[3,3,256]{2,1,0:T(4,128)S(1)}, f32[3,3,256]{2,1,0:T(4,128)}, u32[]{:S(2)}) copy-start(f32[3,3,256]{2,1,0:T(4,128)} %param.11) | copy-start | bytes 27652
  11.5 186.0 %all-to-all-start = ((bf16[64,64,768]{2,1,0:T(8,128)(2,1)}), bf16[64,64,768]{2,1,0:T(8,128)(2,1)}, u32[]{:S(2)}, u32[]{:S(2)}) async-start(bf16[64,64,768]{2,1,0:T(8,128)(2,1)} %stack.178), calls=%async_computation | async-start | bytes 12582912 | tf_op jit(solution)/shard_map/all_to_all | solution.py:134
  23.9 17.4 %collective-permute-start.1 = (bf16[64,256]{1,0:T(8,128)(2,1)S(1)}, bf16[64,256]{1,0:T(8,128)(2,1)S(1)}, u32[]{:S(2)}, u32[]{:S(2)}) collective-permute-start(bf16[64,256]{1,0:T(8,128)(2,1)S(1)} %bitcast.214), channel_id=1, source_target_pairs={{0,128},{4,132},{8,136},{12,140},{16,144},{20,148},{24,152},{28,15... | collective-permute-start | bytes 98312 | tf_op jit(solution)/shard_map/ppermute | solution.py:25
  41.3 4.9 %collective-permute-start.2 = (bf16[2,64,256]{2,1,0:T(8,128)(2,1)S(1)}, bf16[2,64,256]{2,1,0:T(8,128)(2,1)S(1)}, u32[]{:S(2)}, u32[]{:S(2)}) collective-permute-start(bf16[2,64,256]{2,1,0:T(8,128)(2,1)S(1)} %maximum_select_fusion.8), channel_id=1, source_target_pairs={{0,64},{4,68},{8,72},{12,76},{16,80},{20,84},{24,88},{28,92},{32,9... | collective-permute-start | bytes 196616 | tf_op jit(solution)/shard_map/ppermute | solution.py:25
  46.2 124.2 %collective-permute-start.3 = (bf16[2,2,64,256]{3,2,0,1:T(8,128)(2,1)S(1)}, bf16[2,2,64,256]{3,2,0,1:T(8,128)(2,1)S(1)}, u32[]{:S(2)}, u32[]{:S(2)}) collective-permute-start(bf16[2,2,64,256]{3,2,0,1:T(8,128)(2,1)S(1)} %maximum_select_fusion.7), channel_id=1, source_target_pairs={{0,32},{4,36},{8,40},{12,44},{16,48},{20,52},{24,56},{28,60},{32,0... | collective-permute-start | bytes 393224 | tf_op jit(solution)/shard_map/ppermute | solution.py:25
  48.7 136.7 %copy-start.23 = (f32[128,256]{1,0:T(8,128)S(1)}, f32[128,256]{1,0:T(8,128)}, u32[]{:S(2)}) copy-start(f32[128,256]{1,0:T(8,128)} %param.12) | copy-start | bytes 393220
  170.4 12.3 %collective-permute-start.4 = (bf16[2,2,2,64,256]{4,3,0,1,2:T(8,128)(2,1)S(1)}, bf16[2,2,2,64,256]{4,3,0,1,2:T(8,128)(2,1)S(1)}, u32[]{:S(2)}, u32[]{:S(2)}) collective-permute-start(bf16[2,2,2,64,256]{4,3,0,1,2:T(8,128)(2,1)S(1)} %maximum_select_fusion.6), channel_id=1, source_target_pairs={{0,16},{4,20},{8,24},{12,28},{16,0},{20,4},{24,8},{28,12},{32,48},... | collective-permute-start | bytes 786440 | tf_op jit(solution)/shard_map/ppermute | solution.py:25
  182.8 11.6 %collective-permute-start.5 = (bf16[2,2,2,2,64,256]{5,4,0,1,2,3:T(8,128)(2,1)S(1)}, bf16[2,2,2,2,64,256]{5,4,0,1,2,3:T(8,128)(2,1)S(1)}, u32[]{:S(2)}, u32[]{:S(2)}) collective-permute-start(bf16[2,2,2,2,64,256]{5,4,0,1,2,3:T(8,128)(2,1)S(1)} %maximum_select_fusion.3), channel_id=1, source_target_pairs={{0,8},{4,12},{8,0},{12,4},{16,24},{20,28},{24,16},{28,20},{32,40},... | collective-permute-start | bytes 1572872 | tf_op jit(solution)/shard_map/ppermute | solution.py:25
  184.0 2.2 copy-start.13
  184.0 2.2 copy-start.15
  186.3 8.4 %copy-start = (bf16[128,4096]{1,0:T(8,128)(2,1)S(1)}, bf16[128,4096]{1,0:T(8,128)(2,1)}, u32[]{:S(2)}) copy-start(bf16[128,4096]{1,0:T(8,128)(2,1)} %param.8) | copy-start | bytes 3145732
  194.5 2.7 collective-permute-start.6
  195.5 12.0 %copy-start.30 = (f32[128]{0:T(128)}, f32[128]{0:T(128)S(1)}, u32[]{:S(2)}) copy-start(f32[128]{0:T(128)S(1)} %get-tuple-element.53) | copy-start | bytes 1540
  197.3 10.2 %copy-start.24 = (f32[4096]{0:T(1024)S(1)}, f32[4096]{0:T(1024)}, u32[]{:S(2)}) copy-start(f32[4096]{0:T(1024)} %param.9) | copy-start | bytes 49156
  197.5 24.4 %all-to-all-start.2 = ((f32[1,256,128]{2,0,1:T(1,128)}), f32[1,256,128]{2,0,1:T(1,128)}, u32[]{:S(2)}, u32[]{:S(2)}) async-start(f32[1,256,128]{2,0,1:T(1,128)} %bitcast.1), calls=%async_computation.2 | async-start | bytes 262144 | tf_op jit(solution)/shard_map/all_to_all | solution.py:52
  207.5 6.5 %copy-start.8 = (bf16[128,4096]{1,0:T(8,128)(2,1)S(1)}, bf16[128,4096]{1,0:T(8,128)(2,1)}, u32[]{:S(2)}) copy-start(bf16[128,4096]{1,0:T(8,128)(2,1)} %param.15) | copy-start | bytes 3145732
  212.0 7.2 %collective-permute-start = (bf16[2,3,256]{2,0,1:T(2,128)(2,1)}, bf16[2,3,256]{2,0,1:T(2,128)(2,1)S(1)}, u32[]{:S(2)}, u32[]{:S(2)}) collective-permute-start(bf16[2,3,256]{2,0,1:T(2,128)(2,1)} %bitcast.7), channel_id=1, source_target_pairs={{0,4},{4,8},{8,12},{12,16},{16,20},{20,24},{24,28},{28,32},{32,36}... | collective-permute-start | bytes 9224 | tf_op jit(solution)/shard_map/ppermute | solution.py:14
  215.5 3.9 %copy-start.9 = (f32[128,256]{1,0:T(8,128)S(1)}, f32[128,256]{1,0:T(8,128)}, u32[]{:S(2)}) copy-start(f32[128,256]{1,0:T(8,128)} %convolution_bitcast_fusion.3) | copy-start | bytes 393220
  221.9 21.1 %all-to-all-start.1 = ((f32[2,256,128]{2,0,1:T(2,128)}), f32[2,256,128]{2,0,1:T(2,128)}, u32[]{:S(2)}, u32[]{:S(2)}) async-start(f32[2,256,128]{2,0,1:T(2,128)} %copy.120), calls=%async_computation.1 | async-start | bytes 524288 | tf_op jit(solution)/shard_map/all_to_all | solution.py:52
  232.5 0.6 copy-start.17
  232.5 0.6 copy-start.19
  243.0 2.7 copy-start.10
  243.0 2.7 copy-start.11
  243.0 2.7 copy-start.12
  245.7 1.1 copy-start.1
  247.0 0.9 copy-start.14
  247.0 0.9 copy-start.16
  247.8 0.8 copy-start.18
  247.8 0.8 copy-start.20
  248.6 27.4 %copy-start.27 = (f32[256]{0:T(256)S(1)}, f32[256]{0:T(256)}, u32[]{:S(2)}) copy-start(f32[256]{0:T(256)} %param.13) | copy-start | bytes 3076
  250.2 20.7 %all-to-all-start.3 = ((f32[64,3,4,128]{3,2,1,0:T(4,128)}), f32[64,3,4,128]{3,2,1,0:T(4,128)}, u32[]{:S(2)}, u32[]{:S(2)}) async-start(f32[64,3,4,128]{3,2,1,0:T(4,128)} %copy.131), calls=%async_computation.3 | async-start | bytes 786432 | tf_op jit(solution)/shard_map/all_to_all | solution.py:60
  256.9 71.0 %reduce-scatter.2.cloned.1.call-start = ((), (), s32[]{:S(2)}) async-start(), calls=%async_computation.5 | async-start | bytes 2785280 | tf_op jit(solution)/shard_map/reduce_scatter | solution.py:213
  277.1 0.8 copy-start.4
  277.1 1.4 copy-start.6
  277.2 0.7 copy-start.2
  278.5 6.4 %collective-permute-start.7 = (f32[2,3,256]{2,0,1:T(2,128)}, f32[2,3,256]{2,0,1:T(2,128)}, u32[]{:S(2)}, u32[]{:S(2)}) collective-permute-start(f32[2,3,256]{2,0,1:T(2,128)} %slice.165), channel_id=1, source_target_pairs={{4,0},{8,4},{12,8},{16,12},{20,16},{24,20},{28,24},{32,28},{36,32}... | collective-permute-start | bytes 18440 | tf_op jit(solution)/shard_map/ppermute | solution.py:14
  283.0 1.9 copy-start.3
  283.0 1.9 copy-start.5
  283.0 1.9 copy-start.7
  284.8 1.2 copy-start.25
  291.3 2.8 copy-start.28
  295.8 33.4 %copy-start.29 = (f32[128]{0:T(128)S(1)}, f32[128]{0:T(128)}, u32[]{:S(2)}) copy-start(f32[128]{0:T(128)} %get-tuple-element.52) | copy-start | bytes 1540
  295.8 33.4 %copy-start.31 = (f32[128]{0:T(128)S(1)}, f32[128]{0:T(128)}, u32[]{:S(2)}) copy-start(f32[128]{0:T(128)} %copy-done.30) | copy-start | bytes 1540
  329.0 12.0 %copy-start.21 = (f32[1,128,64,4]{1,3,0,2:T(4,128)S(1)}, f32[1,128,64,4]{1,3,0,2:T(4,128)}, u32[]{:S(2)}) copy-start(f32[1,128,64,4]{1,3,0,2:T(4,128)} %get-tuple-element.35) | copy-start | bytes 393220
  331.1 9.5 %collective-permute-start.8 = (bf16[1,128,1024]{2,1,0:T(8,128)(2,1)S(1)}, bf16[1,128,1024]{2,1,0:T(8,128)(2,1)S(1)}, u32[]{:S(2)}, u32[]{:S(2)}) collective-permute-start(bf16[1,128,1024]{2,1,0:T(8,128)(2,1)S(1)} %bitcast.193), channel_id=1, source_target_pairs={{0,2},{1,3},{2,0},{3,1},{4,6},{5,7},{6,4},{7,5},{8,10},{9,11},{10,... | collective-permute-start | bytes 786440 | tf_op jit(solution)/shard_map/ppermute | solution.py:25
  340.7 12.8 %collective-permute-start.9 = (bf16[2,1,128,1024]{3,2,1,0:T(8,128)(2,1)S(1)}, bf16[2,1,128,1024]{3,2,1,0:T(8,128)(2,1)S(1)}, u32[]{:S(2)}, u32[]{:S(2)}) collective-permute-start(bf16[2,1,128,1024]{3,2,1,0:T(8,128)(2,1)S(1)} %maximum_select_fusion.5), channel_id=1, source_target_pairs={{0,1},{1,0},{2,3},{3,2},{4,5},{5,4},{6,7},{7,6},{8,9},{9,8},{10,11... | collective-permute-start | bytes 1572872 | tf_op jit(solution)/shard_map/ppermute | solution.py:25
Sparse Core Ops, SparseCore 0:
  295.9 31.8 reduce-scatter.1
